TPU v7x, 32 devices: a whole 2x2x4 slice. The times are simulated.
32 devices in a mesh: groups: 2 (over y), blk: 4 (over z), pool: 4 (over x, core).
Axes of the slice: x: 2, y: 2, z: 4, core: 2. Of those that a mesh axis runs over, the one named last changes fastest.
Arguments:
- q_new: bfloat16 [1024, 8192], P(('groups', 'blk'), 'pool'), parts along dimension 0, may hold values from -64 to 64
- kv_new: bfloat16 [1024, 8, 256], P(('groups', 'blk'), 'pool'), parts along dimension 0, may hold values from -7 to 7
- kv_cache: bfloat16 [256, 8, 128, 256], P(('groups', 'blk'), 'pool'), parts along dimension 0, may hold values from -4.5 to 4.5
- page_table: int32 [16], P('groups'), parts along dimension 0, may hold values from 0 to 127, as said below
- block_offsets: int32 [8], P('groups'), parts along dimension 0, may hold values from 0 to 3, each once
Outputs:
- attended: bfloat16 [1024, 8192], P(('groups', 'blk'), 'pool'), parts along dimension 0
There are 2 independent parts, one for each index of `groups`. A program takes and returns all parts, laid end to end along the dimension named above; each array names one. Nothing has to cross between parts.
Inputs may be any that keep to these rules, and one draw needn't show every extreme that they name: `page_table`: distinct slots; slot s lies on blk index s // 32; at most 4 entries lie on the slots of one blk index, and exactly 4 on some blk index.
All inputs are finite; a program needn't handle non-finite values.
Results may differ from a plain program's by a relative error of at most 0.0045.
Values may be sent and summed in bfloat16 or wider, within the bound.
No kernel may reach another device: no remote copies, remote signals or barrier semaphores. Data moves between devices by JAX's collectives and lax.ppermute only.
A program may use at most 64 MiB of HBM per device.

v0:
```python
import math
import jax
import jax.numpy as jnp
from jax import lax
from jax.sharding import PartitionSpec as P

CAP = 4


def attend(running, queries, keys, values, visible, head_size):
    maxima, totals, summed = running
    score_scale = 1.0 / math.sqrt(head_size)
    scores = (
        jnp.einsum("gqd,gkd->gqk", queries, keys, preferred_element_type=jnp.float32) * score_scale
    )
    scores = jnp.where(visible, scores, -1e30)
    row_top = jnp.maximum(maxima, jnp.max(scores, axis=2))
    factor = jnp.exp(maxima - row_top)
    weights = jnp.where(visible, jnp.exp(scores - row_top[..., None]), 0.0)
    totals = totals * factor + jnp.sum(weights, axis=2)
    summed = summed * factor[..., None] + jnp.einsum(
        "gqk,gkd->gqd", weights.astype(jnp.bfloat16), values, preferred_element_type=jnp.float32
    )
    return (row_top, totals, summed)


def local(q_new, kv_new, kv_cache, page_table, block_offsets):
    q_rows = q_new.shape[0]
    kv_heads = kv_new.shape[1]
    head_size = kv_new.shape[2] // 2
    group_size = q_new.shape[1] // (head_size * kv_heads)
    slots_dev = kv_cache.shape[0]
    page_len = kv_cache.shape[2]
    npages = page_table.shape[0]
    blocks = lax.axis_size("blk")
    myself = lax.axis_index("blk")
    pg = -(-npages // blocks)
    block_ids = jnp.arange(blocks, dtype=jnp.int32)
    my_offset = jnp.sum(jnp.where(block_ids == myself, block_offsets, 0))
    query_pos = jnp.tile(my_offset * q_rows + jnp.arange(q_rows, dtype=jnp.int32), group_size)
    queries = (
        q_new.reshape(q_rows, kv_heads, group_size, head_size)
        .transpose(1, 2, 0, 3)
        .reshape(kv_heads, group_size * q_rows, head_size)
    )
    query_span = group_size * q_rows
    page_owner = page_table // slots_dev
    owned = page_owner == myself
    page_rank = jnp.cumsum(owned.astype(jnp.int32)) - 1
    local_slot = page_table % slots_dev
    counts = jnp.sum((page_owner[None, :] == block_ids[:, None]).astype(jnp.int32), axis=1)
    per_peer = (CAP + blocks - 1) // blocks
    starts = jnp.cumsum(counts) - counts
    my_start = jnp.sum(jnp.where(block_ids == myself, starts, 0))
    peer_slots = jnp.arange(per_peer, dtype=jnp.int32)[None, :]
    wanted = (block_ids[:, None] - my_start) % blocks + peer_slots * blocks
    picked = owned[None, None, :] & (page_rank[None, None, :] == wanted[..., None])
    chosen = jnp.sum(jnp.where(picked, local_slot[None, None, :], 0), axis=2).reshape(-1)
    sent_pages = kv_cache[chosen].reshape(blocks, per_peer, kv_heads, page_len, 2 * head_size)
    sent_pages = sent_pages.transpose(0, 2, 1, 3, 4).reshape(
        blocks, kv_heads, per_peer * page_len, 2 * head_size
    )
    own_rows = jnp.broadcast_to(
        kv_new.transpose(1, 0, 2)[None], (blocks, kv_heads, q_rows, 2 * head_size)
    )
    payload = jnp.concatenate([sent_pages, own_rows], axis=2)
    received = lax.all_to_all(payload, "blk", split_axis=0, concat_axis=0, tiled=True)
    page_part = received[:, :, : per_peer * page_len]
    page_part = page_part.reshape(blocks, kv_heads, per_peer, page_len, 2 * head_size)
    page_part = page_part.transpose(0, 2, 1, 3, 4).reshape(
        blocks * per_peer, kv_heads, page_len, 2 * head_size
    )
    arriving = (myself - starts[:, None]) % blocks + peer_slots * blocks
    present = (arriving < counts[:, None]).reshape(-1)
    order_rank = jnp.cumsum(present.astype(jnp.int32)) - 1
    choose = present[None, :] & (order_rank[None, :] == jnp.arange(pg, dtype=jnp.int32)[:, None])
    positions = jnp.sum(
        jnp.where(choose, jnp.arange(blocks * per_peer, dtype=jnp.int32)[None, :], 0), axis=1
    )
    compact = page_part[positions]
    compact_valid = jnp.arange(pg, dtype=jnp.int32) * blocks + myself < npages
    gathered = lax.all_gather(compact, "blk", axis=0, tiled=True)
    gathered_valid = (
        jnp.arange(pg, dtype=jnp.int32)[None, :] * blocks + block_ids[:, None] < npages
    ).reshape(-1)
    new_rows = received[:, :, per_peer * page_len :]
    new_rows = new_rows.transpose(1, 0, 2, 3).reshape(kv_heads, blocks * q_rows, 2 * head_size)
    own_pages = compact.transpose(1, 0, 2, 3).reshape(kv_heads, pg * page_len, 2 * head_size)
    entries_a = jnp.concatenate([new_rows, own_pages], axis=1)
    row_source = jnp.repeat(block_ids, q_rows)
    key_pos = jnp.sum(
        jnp.where(row_source[:, None] == block_ids[None, :], block_offsets[None, :], 0), axis=1
    ) * q_rows + jnp.tile(jnp.arange(q_rows, dtype=jnp.int32), blocks)
    visible_new = key_pos[None, :] <= query_pos[:, None]
    visible_own = jnp.broadcast_to(
        jnp.repeat(compact_valid, page_len)[None, :], (query_span, pg * page_len)
    )
    visible_a = jnp.concatenate([visible_new, visible_own], axis=1)[None]
    running = (
        jnp.full((kv_heads, query_span), -1e30, jnp.float32),
        jnp.zeros((kv_heads, query_span), jnp.float32),
        jnp.zeros((kv_heads, query_span, head_size), jnp.float32),
    )
    running = attend(
        running,
        queries,
        entries_a[..., :head_size],
        entries_a[..., head_size:],
        visible_a,
        head_size,
    )
    page_block = jnp.repeat(block_ids, pg)
    use_page = gathered_valid & (page_block != myself)
    entries_b = gathered.transpose(1, 0, 2, 3).reshape(
        kv_heads, blocks * pg * page_len, 2 * head_size
    )
    visible_b = jnp.repeat(use_page, page_len)[None, None, :]
    running = attend(
        running,
        queries,
        entries_b[..., :head_size],
        entries_b[..., head_size:],
        visible_b,
        head_size,
    )
    maxima, totals, summed = running
    attended = (summed / totals[..., None]).astype(jnp.bfloat16)
    attended = attended.reshape(kv_heads, group_size, q_rows, head_size).transpose(2, 0, 1, 3)
    return attended.reshape(q_rows, kv_heads * group_size * head_size)


def solution(mesh):
    return jax.shard_map(
        local,
        mesh=mesh,
        in_specs=(
            P(("groups", "blk"), "pool"),
            P(("groups", "blk"), "pool", None),
            P(("groups", "blk"), "pool", None, None),
            P("groups"),
            P("groups"),
        ),
        out_specs=P(("groups", "blk"), "pool"),
        check_vma=False,
    )
```

profile of v0, /device:TPU:0, one launch (start us, length us, event | category | flops | bytes accessed | tf_op | source)
XLA Modules:
  0.0 97.5 jit_solution(11759745901006424764)
XLA Ops:
  6.5 0.7 and_select_fusion.3
  7.3 0.7 convert_bitcast_fusion
  8.4 1.4 %fusion.35 = (s32[]{:T(128)}, s32[]{:T(128)}) fusion(s32[4]{0:T(128)} %param.9, s32[]{:T(128)S(6)} %axis_index.15, s32[4]{0:T(128)S(1)} %convert_reduce_fusion, s32[4,1]{0,1:T(1,128)S(1)} %reduce-window.22), kind=kLoop, calls=%fused_computation.78 | loop fusion | flops 22 | bytes 60 | tf_op jit(solution)/shard_map/reduce_sum | solution.py:39
  9.8 0.7 and_select_fusion.4
  10.5 0.2 select_reduce_fusion.1
  10.7 0.9 copy.22
  11.6 2.8 %gather_fusion = bf16[4,2,128,256]{3,2,1,0:T(8,128)(2,1)S(1)} fusion(bf16[32,2,128,256]{3,2,1,0:T(8,128)(2,1)} %param.7, s32[1024]{0:T(1024)S(1)} %pad_clamp_fusion.1), kind=kCustom, calls=%fused_computation | custom fusion | bytes 1048592 | tf_op jit(solution)/shard_map/gather | solution.py:59
  14.4 1.1 %pad_maximum_fusion = bf16[4,2,256,256]{3,2,1,0:T(8,128)(2,1)} fusion(bf16[4,2,128,256]{3,2,1,0:T(8,128)(2,1)S(1)} %broadcast_in_dim.150, bf16[4,2,128,256]{3,2,1,0:T(8,128)(2,1)S(1)} %gather_fusion), kind=kLoop, calls=%fused_computation.23 | loop fusion | flops 2097152 | bytes 2097152 | tf_op jit(solution)/shard_map/concatenate | solution.py:66
  15.5 6.3 %all-to-all-start = ((bf16[4,2,256,256]{3,2,1,0:T(8,128)(2,1)}), bf16[4,2,256,256]{3,2,1,0:T(8,128)(2,1)S(1)}, u32[]{:S(2)}, u32[]{:S(2)}) async-start(bf16[4,2,256,256]{3,2,1,0:T(8,128)(2,1)} %pad_maximum_fusion), calls=%async_computation | async-start | bytes 2097152 | tf_op jit(solution)/shard_map/all_to_all | solution.py:67
  23.4 24.1 %all-to-all-done = bf16[4,2,256,256]{3,2,1,0:T(8,128)(2,1)S(1)} async-done(((bf16[4,2,256,256]{3,2,1,0:T(8,128)(2,1)}), bf16[4,2,256,256]{3,2,1,0:T(8,128)(2,1)S(1)}, u32[]{:S(2)}, u32[]{:S(2)}) %all-to-all-start) | async-done | bytes 1048608 | tf_op jit(solution)/shard_map/all_to_all | solution.py:67
  47.7 1.3 %gather_fusion.1 = bf16[2,2,128,256]{3,2,1,0:T(8,128)(2,1)} fusion(bf16[4,2,128,256]{3,2,1,0:T(8,128)(2,1)S(1)} %get-tuple-element.10, s32[1024]{0:T(1024)S(1)} %pad_clamp_fusion), kind=kCustom, calls=%fused_computation.1 | custom fusion | bytes 524296 | tf_op jit(solution)/shard_map/gather | solution.py:80
  49.0 0.4 broadcast_compare_fusion
  49.4 0.4 pad_add_fusion
  49.8 1.0 copy.24
  50.8 4.0 %fusion.4 = (f32[2,1024]{1,0:T(2,128)S(1)}, f32[2,768,1024]{2,1,0:T(8,128)}) fusion(pred[1024,768]{0,1:T(8,128)(4,1)S(1)} %pad_add_fusion, bf16[2,1024,128]{2,1,0:T(8,128)(2,1)S(1)} %bitcast.92, bf16[2,512,256]{2,1,0:T(8,128)(2,1)S(1)} %bitcast.98, bf16[2,256,256]{2,1,0:T(8,128)(2,1)S(1)} %bitcast.101), kind=kOutput, calls=%fused_computation.11 | convolution fusion | flops 408156160 | bytes 8396800 | tf_op jit(solution)/shard_map/gqd,gkd->gqk/dot_general | solution.py:14
  54.9 21.3 %all-gather.3.cloned.1.call-done = bf16[8,2,128,256]{3,2,1,0:T(8,128)(2,1)} async-done(((bf16[2,2,128,256]{3,2,1,0:T(8,128)(2,1)}), bf16[8,2,128,256]{3,2,1,0:T(8,128)(2,1)}) %all-gather.3.cloned.1.call-update) | async-done | bytes 1048592 | tf_op jit(solution)/shard_map/all_gather | solution.py:82
  76.1 1.3 %copy.27 = bf16[2,8,128,256]{3,2,1,0:T(8,128)(2,1)S(1)} copy(bf16[2,8,128,256]{3,2,0,1:T(8,128)(2,1)} %bitcast.96) | data formatting | bytes 2097152 | tf_op jit(solution)/shard_map/transpose | solution.py:114
  77.5 1.9 %bitcast_reduce_fusion = (f32[2,1024]{1,0:T(2,128)S(1)}, f32[2,1024,1024]{2,1,0:T(8,128)S(1)}) fusion(pred[1024]{0:T(1024)(128)(4,1)S(1)} %broadcast_bitcast_fusion.1, bf16[2,1024,128]{2,1,0:T(8,128)(2,1)S(1)} %bitcast.93, bf16[2,1024,256]{2,1,0:T(8,128)(2,1)S(1)} %bitcast.89), kind=kOutput, calls=%fused_computation.3 | convolution fusion | flops 543160320 | bytes 9446400 | tf_op jit(solution)/shard_map/gqd,gkd->gqk/dot_general | solution.py:14
  79.4 2.5 %fusion.2 = f32[2,1024]{1,0:T(2,128)S(1)} fusion(f32[2,1024,1024]{2,1,0:T(8,128)S(1)} %get-tuple-element.18, f32[2,1024]{1,0:T(2,128)S(1)} %get-tuple-element.13, pred[1024]{0:T(1024)(128)(4,1)S(1)} %broadcast_bitcast_fusion.1), kind=kLoop, calls=%fused_computation.9 | loop fusion | flops 10483712 | bytes 8406016 | tf_op jit(solution)/shard_map/reduce_sum | solution.py:20
  81.9 1.7 %fusion.5 = f32[2,1024]{1,0:T(2,128)S(1)} fusion(f32[2,768,1024]{2,1,0:T(8,128)S(1)} %bitcast.88, f32[2,1024]{1,0:T(2,128)S(1)} %get-tuple-element.14, pred[1024,768]{0,1:T(8,128)(4,1)S(1)} %pad_add_fusion), kind=kLoop, calls=%fused_computation.12 | loop fusion | flops 7862272 | bytes 7094272 | tf_op jit(solution)/shard_map/reduce_sum | solution.py:20
  83.6 2.8 %fusion.20 = f32[2,1024,128]{2,1,0:T(8,128)S(1)} fusion(f32[2,768,1024]{2,1,0:T(8,128)S(1)} %bitcast.88, f32[2,1024]{1,0:T(2,128)S(1)} %get-tuple-element.14, pred[1024,768]{0,1:T(8,128)(4,1)S(1)} %pad_add_fusion, f32[2,1024]{1,0:T(2,128)S(1)} %get-tuple-element.6, f32[2,1024]{1,0:T(2,128)S(1)} %get-tuple-element.12, ...), kind=kOutput, calls=%fused_computation.22 | convolution fusion | flops 411828224 | bytes 8937472 | tf_op jit(solution)/shard_map/gqk,gkd->gqd/dot_general | solution.py:21
  86.4 3.0 %divide_convert_fusion = bf16[2,1024,128]{2,1,0:T(8,128)(2,1)S(1)} fusion(f32[2,1024,128]{2,1,0:T(8,128)S(1)} %fusion.20, f32[2,1024,1024]{2,1,0:T(8,128)S(1)} %get-tuple-element.18, f32[2,1024]{1,0:T(2,128)S(1)} %get-tuple-element.13, pred[1024]{0:T(1024)(128)(4,1)S(1)} %broadcast_bitcast_fusion.1, bf16[2,1024,256]{2,1,0:T(8,128)(2,1)S(1)} %bitcast.90, ...), kind=kOutput, calls=%fused_computation.24 | convolution fusion | flops 548143104 | bytes 10504192 | tf_op jit(solution)/shard_map/gqk,gkd->gqd/dot_general | solution.py:21
  89.4 0.3 copy.29
  89.8 0.9 copy.35
  (43 shorter events, 1.7 us)
Async XLA Ops:
  6.5 16.8 %copy-start.1 = (s32[4]{0:T(128)S(1)}, s32[4]{0:T(128)}, u32[]{:S(2)}) copy-start(s32[4]{0:T(128)} %param.9) | copy-start | bytes 52
  6.5 15.6 %copy-start = (bf16[128,2048]{1,0:T(8,128)(2,1)S(1)}, bf16[128,2048]{1,0:T(8,128)(2,1)}, u32[]{:S(2)}) copy-start(bf16[128,2048]{1,0:T(8,128)(2,1)} %param.5) | copy-start | bytes 1572868
  15.5 32.0 %all-to-all-start = ((bf16[4,2,256,256]{3,2,1,0:T(8,128)(2,1)}), bf16[4,2,256,256]{3,2,1,0:T(8,128)(2,1)S(1)}, u32[]{:S(2)}, u32[]{:S(2)}) async-start(bf16[4,2,256,256]{3,2,1,0:T(8,128)(2,1)} %pad_maximum_fusion), calls=%async_computation | async-start | bytes 2097152 | tf_op jit(solution)/shard_map/all_to_all | solution.py:67
  21.8 54.3 %all-gather.3.cloned.1.call-start = ((), (), s32[]{:S(2)}) async-start(), calls=%async_computation.1 | async-start | bytes 1310720 | tf_op jit(solution)/shard_map/all_gather | solution.py:82
  77.4 4.5 %slice-start = ((s8[6291456]{0:T(1024)(128)(4,1)}), s8[4194304]{0:T(1024)(128)(4,1)S(1)}, s32[]{:S(2)}) async-start(s8[6291456]{0:T(1024)(128)(4,1)} %bitcast.87), calls=%async_computation.2 | async-start | bytes 8388608
  77.4 4.5 %slice-start.1 = ((s8[6291456]{0:T(1024)(128)(4,1)}), s8[2097152]{0:T(1024)(128)(4,1)S(1)}, s32[]{:S(2)}) async-start(s8[6291456]{0:T(1024)(128)(4,1)} %bitcast.87), calls=%async_computation.3 | async-start | bytes 4194304
Sparse Core Ops, SparseCore 0:
  49.1 27.0 all-gather.2
where the time goes:
time: 97.9 us; the launch traced here: 97.5 us
  waiting for transfers between devices  45.4 us (46%)
  between operations  14.3 us (15%)
  matrix products  11.7 us (12%)
  other arithmetic  10.6 us (11%)
  local copies, waits for them, and re-layouts  9.17 us (9%)
  starting transfers between devices  6.32 us (6%)
    all_to_all x1, waiting for transfers between devices, local(): lax.all_to_all(payload, 'blk', split_axis=0, concat_axis=0, tiled=True)  24.1 us
    all_gather x1, waiting for transfers between devices, local(): gathered = lax.all_gather(compact, 'blk', axis=0, tiled=True)  21.3 us
    all_to_all x1, starting transfers between devices, local(): lax.all_to_all(payload, 'blk', split_axis=0, concat_axis=0, tiled=True)  6.32 us
    dot_general x2, matrix products, attend(): jnp.einsum('gqd,gkd->gqk', queries, keys, preferred_element_type=jnp.floa...  5.92 us
    dot_general x2, matrix products, attend(): jnp.einsum('gqk,gkd->gqd', weights.astype(jnp.bfloat16), values, preferre...  5.81 us
    reduce_sum x2, other arithmetic, attend(): totals = totals * factor + jnp.sum(weights, axis=2)  4.16 us
    gather x1, local copies, waits for them, and re-layouts, local(): kv_cache[chosen]  2.77 us
  transfers between devices with their start and end apart: 2, of which 2 were waited for; matrix products, arithmetic and copies ran while one was open for 7% of the time, Pallas kernels for 0%

commit v1 on v0

--- a/solution.py
+++ b/solution.py
@@ -79,7 +79,12 @@
     )
     compact = page_part[positions]
     compact_valid = jnp.arange(pg, dtype=jnp.int32) * blocks + myself < npages
-    gathered = lax.all_gather(compact, "blk", axis=0, tiled=True)
+    ring = [compact]
+    for hop in range(3):
+        ring.append(lax.ppermute(ring[-1], "blk", [(dev, (dev + 1) % 4) for dev in range(4)]))
+    gathered = jnp.roll(
+        jnp.concatenate(ring[::-1], axis=0), (lax.axis_index("blk") + 1) * ring[0].shape[0], axis=0
+    )
     gathered_valid = (
         jnp.arange(pg, dtype=jnp.int32)[None, :] * blocks + block_ids[:, None] < npages
     ).reshape(-1)

time: 97.9 us -> 81.4 us (0.83)
  between operations: 14.3 us -> 0.93 us
  local copies, waits for them, and re-layouts: 9.17 us -> 6.55 us
  matrix products: 11.7 us -> 9.38 us
  waiting for transfers between devices: 45.4 us -> 46.5 us
    ppermute x0 -> x3, waiting for transfers between devices: none -> 22.8 us  [local(): lax.ppermute(ring[-1], 'blk', [(dev, (dev + 1) % 4) for dev in range(4)])]
    all_gather x1 -> x0, waiting for transfers between devices: 21.3 us -> none  [local(): gathered = lax.all_gather(compact, 'blk', axis=0, tiled=True)]
    dot_general x2, matrix products: 5.92 us -> 3.29 us  [attend(): jnp.einsum('gqd,gkd->gqk', queries, keys, preferred_element_type=jnp.floa...]
    transpose x1 -> x2, local copies, waits for them, and re-layouts: 1.29 us -> 0.19 us  [local(): gathered.transpose(1, 0, 2, 3)]
  transfers between devices with their start and end apart: 2 -> 4, of which waited for: 2 -> 4; matrix products, arithmetic and copies ran while one was open for 7% -> 5% of each run, Pallas kernels for 0% -> 0%
where the time goes in v1:
time: 81.4 us; the launch traced here: 81.1 us
  waiting for transfers between devices  46.5 us (57%)
  other arithmetic  11.4 us (14%)
  matrix products  9.38 us (12%)
  local copies, waits for them, and re-layouts  6.55 us (8%)
  starting transfers between devices  6.38 us (8%)
  between operations  0.93 us (1%)
    all_to_all x1, waiting for transfers between devices, local(): lax.all_to_all(payload, 'blk', split_axis=0, concat_axis=0, tiled=True)  23.8 us
    ppermute x3, waiting for transfers between devices, local(): lax.ppermute(ring[-1], 'blk', [(dev, (dev + 1) % 4) for dev in range(4)])  22.8 us
    all_to_all x1, starting transfers between devices, local(): lax.all_to_all(payload, 'blk', split_axis=0, concat_axis=0, tiled=True)  6.32 us
    dot_general x2, matrix products, attend(): jnp.einsum('gqk,gkd->gqd', weights.astype(jnp.bfloat16), values, preferre...  6.09 us
    reduce_sum x2, other arithmetic, attend(): totals = totals * factor + jnp.sum(weights, axis=2)  4.22 us
    dot_general x2, matrix products, attend(): jnp.einsum('gqd,gkd->gqk', queries, keys, preferred_element_type=jnp.floa...  3.29 us
    gather x1, local copies, waits for them, and re-layouts, local(): kv_cache[chosen]  2.77 us
  transfers between devices with their start and end apart: 4, of which 4 were waited for; matrix products, arithmetic and copies ran while one was open for 5% of the time, Pallas kernels for 0%

profile of v1, /device:TPU:0, one launch (start us, length us, event | category | flops | bytes accessed | tf_op | source)
XLA Modules:
  0.0 81.1 jit_solution(3042054616523214130)
XLA Ops:
  0.0 0.7 and_select_fusion.3
  0.7 0.7 convert_bitcast_fusion
  1.9 1.4 %fusion.35 = (s32[]{:T(128)}, s32[]{:T(128)}) fusion(s32[4]{0:T(128)} %param.9, s32[]{:T(128)S(6)} %axis_index.19, s32[4]{0:T(128)S(1)} %convert_reduce_fusion, s32[4,1]{0,1:T(1,128)S(1)} %reduce-window.22), kind=kLoop, calls=%fused_computation.87 | loop fusion | flops 22 | bytes 60 | tf_op jit(solution)/shard_map/reduce_sum | solution.py:39
  3.3 0.7 and_select_fusion.4
  4.2 0.9 %copy.14 = bf16[2,128,256]{2,1,0:T(8,128)(2,1)S(1)} copy(bf16[2,128,256]{2,0,1:T(2,128)(2,1)} %bitcast.101) | data formatting | bytes 262144 | tf_op jit(solution)/shard_map/transpose | solution.py:64
  5.1 2.8 %gather_fusion = bf16[4,2,128,256]{3,2,1,0:T(8,128)(2,1)S(1)} fusion(bf16[32,2,128,256]{3,2,1,0:T(8,128)(2,1)} %param.7, s32[1024]{0:T(1024)S(1)} %pad_clamp_fusion.1), kind=kCustom, calls=%fused_computation | custom fusion | bytes 1048592 | tf_op jit(solution)/shard_map/gather | solution.py:59
  7.9 1.1 %pad_maximum_fusion = bf16[4,2,256,256]{3,2,1,0:T(8,128)(2,1)} fusion(bf16[4,2,128,256]{3,2,1,0:T(8,128)(2,1)S(1)} %broadcast_in_dim.150, bf16[4,2,128,256]{3,2,1,0:T(8,128)(2,1)S(1)} %gather_fusion), kind=kLoop, calls=%fused_computation.23 | loop fusion | flops 2097152 | bytes 2097152 | tf_op jit(solution)/shard_map/concatenate | solution.py:66
  9.0 6.3 %all-to-all-start = ((bf16[4,2,256,256]{3,2,1,0:T(8,128)(2,1)}), bf16[4,2,256,256]{3,2,1,0:T(8,128)(2,1)S(1)}, u32[]{:S(2)}, u32[]{:S(2)}) async-start(bf16[4,2,256,256]{3,2,1,0:T(8,128)(2,1)} %pad_maximum_fusion), calls=%async_computation | async-start | bytes 2097152 | tf_op jit(solution)/shard_map/all_to_all | solution.py:67
  16.4 0.7 select_reduce_fusion
  17.3 23.8 %all-to-all-done = bf16[4,2,256,256]{3,2,1,0:T(8,128)(2,1)S(1)} async-done(((bf16[4,2,256,256]{3,2,1,0:T(8,128)(2,1)}), bf16[4,2,256,256]{3,2,1,0:T(8,128)(2,1)S(1)}, u32[]{:S(2)}, u32[]{:S(2)}) %all-to-all-start) | async-done | bytes 1048608 | tf_op jit(solution)/shard_map/all_to_all | solution.py:67
  41.1 0.6 gather_fusion.1
  42.1 0.4 broadcast_compare_fusion
  42.5 8.3 %collective-permute-done = bf16[2,2,128,256]{3,2,1,0:T(8,128)(2,1)S(1)} collective-permute-done((bf16[2,2,128,256]{3,2,1,0:T(8,128)(2,1)S(1)}, bf16[2,2,128,256]{3,2,1,0:T(8,128)(2,1)S(1)}, u32[]{:S(2)}, u32[]{:S(2)}) %collective-permute-start) | collective-permute-done | bytes 262176 | tf_op jit(solution)/shard_map/ppermute | solution.py:84
  50.8 0.4 pad_add_fusion
  51.3 7.7 %collective-permute-done.1 = bf16[2,2,128,256]{3,2,1,0:T(8,128)(2,1)S(1)} collective-permute-done((bf16[2,2,128,256]{3,2,1,0:T(8,128)(2,1)S(1)}, bf16[2,2,128,256]{3,2,1,0:T(8,128)(2,1)S(1)}, u32[]{:S(2)}, u32[]{:S(2)}) %collective-permute-start.1) | collective-permute-done | bytes 262176 | tf_op jit(solution)/shard_map/ppermute | solution.py:84
  59.0 1.4 %fusion.4 = (f32[2,1024]{1,0:T(2,128)S(1)}, f32[2,768,1024]{2,1,0:T(8,128)S(1)}) fusion(pred[1024,768]{0,1:T(8,128)(4,1)S(1)} %pad_add_fusion, bf16[2,1024,128]{2,1,0:T(8,128)(2,1)S(1)} %bitcast.91, bf16[2,512,256]{2,1,0:T(8,128)(2,1)S(1)} %bitcast.96, bf16[2,256,256]{2,1,0:T(8,128)(2,1)S(1)} %bitcast.99), kind=kOutput, calls=%fused_computation.11 | convolution fusion | flops 408156160 | bytes 8396800 | tf_op jit(solution)/shard_map/gqd,gkd->gqk/dot_general | solution.py:14
  60.4 6.8 %collective-permute-done.2 = bf16[2,2,128,256]{3,2,1,0:T(8,128)(2,1)S(1)} collective-permute-done((bf16[2,2,128,256]{3,2,1,0:T(8,128)(2,1)S(1)}, bf16[2,2,128,256]{3,2,1,0:T(8,128)(2,1)S(1)}, u32[]{:S(2)}, u32[]{:S(2)}) %collective-permute-start.2) | collective-permute-done | bytes 262176 | tf_op jit(solution)/shard_map/ppermute | solution.py:84
  67.6 1.9 %bitcast_reduce_fusion = (f32[2,1024]{1,0:T(2,128)S(1)}, f32[2,1024,1024]{2,1,0:T(8,128)S(1)}) fusion(pred[1024]{0:T(1024)(128)(4,1)S(1)} %broadcast_bitcast_fusion.1, bf16[2,1024,128]{2,1,0:T(8,128)(2,1)S(1)} %bitcast.92, bf16[2,1024,256]{2,1,0:T(8,128)(2,1)S(1)} %bitcast.89), kind=kOutput, calls=%fused_computation.3 | convolution fusion | flops 543160320 | bytes 9446400 | tf_op jit(solution)/shard_map/gqd,gkd->gqk/dot_general | solution.py:14
  69.5 2.6 %fusion.2 = f32[2,1024]{1,0:T(2,128)S(1)} fusion(f32[2,1024,1024]{2,1,0:T(8,128)S(1)} %get-tuple-element.18, f32[2,1024]{1,0:T(2,128)S(1)} %get-tuple-element.13, pred[1024]{0:T(1024)(128)(4,1)S(1)} %broadcast_bitcast_fusion.1), kind=kLoop, calls=%fused_computation.9 | loop fusion | flops 10483712 | bytes 8406016 | tf_op jit(solution)/shard_map/reduce_sum | solution.py:20
  72.1 1.7 %fusion.5 = f32[2,1024]{1,0:T(2,128)S(1)} fusion(f32[2,768,1024]{2,1,0:T(8,128)S(1)} %get-tuple-element.16, f32[2,1024]{1,0:T(2,128)S(1)} %get-tuple-element.14, pred[1024,768]{0,1:T(8,128)(4,1)S(1)} %pad_add_fusion), kind=kLoop, calls=%fused_computation.12 | loop fusion | flops 7862272 | bytes 7094272 | tf_op jit(solution)/shard_map/reduce_sum | solution.py:20
  73.7 2.9 %fusion.20 = f32[2,1024,128]{2,1,0:T(8,128)S(1)} fusion(f32[2,768,1024]{2,1,0:T(8,128)S(1)} %get-tuple-element.16, f32[2,1024]{1,0:T(2,128)S(1)} %get-tuple-element.14, pred[1024,768]{0,1:T(8,128)(4,1)S(1)} %pad_add_fusion, f32[2,1024]{1,0:T(2,128)S(1)} %get-tuple-element.6, f32[2,1024]{1,0:T(2,128)S(1)} %get-tuple-element.12, ...), kind=kOutput, calls=%fused_computation.22 | convolution fusion | flops 411828224 | bytes 8937472 | tf_op jit(solution)/shard_map/gqk,gkd->gqd/dot_general | solution.py:21
  76.7 3.2 %divide_convert_fusion = bf16[2,1024,128]{2,1,0:T(8,128)(2,1)S(1)} fusion(f32[2,1024,128]{2,1,0:T(8,128)S(1)} %fusion.20, f32[2,1024,1024]{2,1,0:T(8,128)S(1)} %get-tuple-element.18, f32[2,1024]{1,0:T(2,128)S(1)} %get-tuple-element.13, pred[1024]{0:T(1024)(128)(4,1)S(1)} %broadcast_bitcast_fusion.1, bf16[2,1024,256]{2,1,0:T(8,128)(2,1)S(1)} %bitcast.90, ...), kind=kOutput, calls=%fused_computation.24 | convolution fusion | flops 548143104 | bytes 10504192 | tf_op jit(solution)/shard_map/gqk,gkd->gqd/dot_general | solution.py:21
  79.8 0.3 copy.21
  80.2 0.9 %copy.27 = bf16[16,8,16,128]{3,1,2,0:T(8,128)(2,1)} copy(bf16[16,8,16,128]{3,2,1,0:T(8,128)(2,1)S(1)} %bitcast.93) | data formatting | bytes 1048576
  (48 shorter events, 2.2 us)
Async XLA Ops:
  0.0 41.8 %copy-start = (bf16[128,2048]{1,0:T(8,128)(2,1)S(1)}, bf16[128,2048]{1,0:T(8,128)(2,1)}, u32[]{:S(2)}) copy-start(bf16[128,2048]{1,0:T(8,128)(2,1)} %param.5) | copy-start | bytes 1572868
  9.0 32.0 %all-to-all-start = ((bf16[4,2,256,256]{3,2,1,0:T(8,128)(2,1)}), bf16[4,2,256,256]{3,2,1,0:T(8,128)(2,1)S(1)}, u32[]{:S(2)}, u32[]{:S(2)}) async-start(bf16[4,2,256,256]{3,2,1,0:T(8,128)(2,1)} %pad_maximum_fusion), calls=%async_computation | async-start | bytes 2097152 | tf_op jit(solution)/shard_map/all_to_all | solution.py:67
  41.7 9.1 %collective-permute-start = (bf16[2,2,128,256]{3,2,1,0:T(8,128)(2,1)S(1)}, bf16[2,2,128,256]{3,2,1,0:T(8,128)(2,1)S(1)}, u32[]{:S(2)}, u32[]{:S(2)}) collective-permute-start(bf16[2,2,128,256]{3,2,1,0:T(8,128)(2,1)S(1)} %gather_fusion.1), channel_id=1, source_target_pairs={{0,4},{4,8},{8,12},{12,0},{1,5},{5,9},{9,13},{13,1},{2,6},{6,10},{... | collective-permute-start | bytes 786440 | tf_op jit(solution)/shard_map/ppermute | solution.py:84
  50.8 8.2 %collective-permute-start.1 = (bf16[2,2,128,256]{3,2,1,0:T(8,128)(2,1)S(1)}, bf16[2,2,128,256]{3,2,1,0:T(8,128)(2,1)S(1)}, u32[]{:S(2)}, u32[]{:S(2)}) collective-permute-start(bf16[2,2,128,256]{3,2,1,0:T(8,128)(2,1)S(1)} %collective-permute-done), channel_id=1, source_target_pairs={{0,4},{4,8},{8,12},{12,0},{1,5},{5,9},{9,13},{13,1},{2,6},{6,10},{... | collective-permute-start | bytes 786440 | tf_op jit(solution)/shard_map/ppermute | solution.py:84
  59.0 8.2 %collective-permute-start.2 = (bf16[2,2,128,256]{3,2,1,0:T(8,128)(2,1)S(1)}, bf16[2,2,128,256]{3,2,1,0:T(8,128)(2,1)S(1)}, u32[]{:S(2)}, u32[]{:S(2)}) collective-permute-start(bf16[2,2,128,256]{3,2,1,0:T(8,128)(2,1)S(1)} %collective-permute-done.1), channel_id=1, source_target_pairs={{0,4},{4,8},{8,12},{12,0},{1,5},{5,9},{9,13},{13,1},{2,6},{6,10},{... | collective-permute-start | bytes 786440 | tf_op jit(solution)/shard_map/ppermute | solution.py:84
